TPU v7x, 32 devices: a whole 2x2x4 slice. The times are simulated.
32 devices in a mesh: ckpt: 2 (over x), train: 4 (over z), tensor: 4 (over y, core).
Axes of the slice: x: 2, y: 2, z: 4, core: 2. Of those that a mesh axis runs over, the one named last changes fastest.
Arguments:
- hidden: bfloat16 [2, 2048, 28672], P('ckpt', 'train', 'tensor'), may hold values from -6 to 6
- out_grads: bfloat16 [2, 2048, 8192], P('ckpt', 'train', 'tensor'), may hold values from -6 to 6
- proj_in: bfloat16 [64, 28672], P(None, 'tensor'), may hold values from -0.03125 to 0.03125
- proj_out: bfloat16 [64, 8192], P(None, 'tensor'), may hold values from -0.0625 to 0.0625
- test_grads: bfloat16 [2, 64, 4096], P('ckpt', ('train', 'tensor')), may hold values from -6 to 6
- step_weights: int32 [2], P('ckpt'), may hold values from 1 to 4
Outputs:
- scores: float32 [16, 4, 16], P('train', None, 'tensor')
All inputs are finite; a program needn't handle non-finite values.
Results may differ from a plain program's by a relative error of at most 0.0029.
Values may be sent and summed in bfloat16 or wider, within the bound.
No kernel may reach another device: no remote copies, remote signals or barrier semaphores. Data moves between devices by JAX's collectives and lax.ppermute only.
A program may use at most 64 MiB of HBM per device.

v0:
```python
import math
import jax
import jax.numpy as jnp
from jax import lax
from jax.sharding import PartitionSpec as P

KIN = 64
KOUT = 64
SEQ = 128


def outer_grads(sides):
    blocks = sides.reshape(-1, SEQ, KIN + KOUT)
    left = blocks[:, :, :KIN]
    right = blocks[:, :, KIN:]
    outer = jnp.einsum("sto,sti->soi", right, left, precision=lax.Precision.HIGHEST)
    return outer.reshape(-1, KIN * KOUT).astype(jnp.bfloat16)


def body(hidden, out_grads, proj_in, proj_out, test_grads, step_weights):
    train_count = lax.axis_size("train")
    h_local = hidden[0]
    g_local = out_grads[0]
    contract = (((1,), (1,)), ((), ()))
    left = lax.dot_general(h_local, proj_in, contract, preferred_element_type=jnp.float32)
    right = lax.dot_general(g_local, proj_out, contract, preferred_element_type=jnp.float32)
    shared = lax.psum_scatter(
        jnp.concatenate([left, right], axis=1), "tensor", scatter_dimension=0, tiled=True
    )
    own = outer_grads(shared)
    train_block = lax.all_gather(own, "tensor", axis=0, tiled=True)
    tests = test_grads[0]
    width = tests.shape[0]
    examples = train_block.shape[0]
    table = lax.dot_general(
        train_block,
        lax.all_gather(test_grads, "train", axis=1, tiled=True)[0],
        contract,
        preferred_element_type=jnp.float32,
    )
    scale = 1.0 / math.sqrt(SEQ * KIN * KOUT)
    weight = step_weights[0].astype(jnp.float32) * scale
    total = lax.psum(table * weight, "ckpt")
    return total.reshape(examples, train_count, width)


def solution(mesh):
    placed = (
        P("ckpt", "train", "tensor"),
        P("ckpt", "train", "tensor"),
        P(None, "tensor"),
        P(None, "tensor"),
        P("ckpt", ("train", "tensor"), None),
        P("ckpt"),
    )
    return jax.shard_map(
        body, mesh=mesh, in_specs=placed, out_specs=P("train", None, "tensor"), check_vma=False
    )
```

profile of v0, /device:TPU:0, one launch (start us, length us, event | category | flops | bytes accessed | tf_op | source)
XLA Modules:
  0.0 55.8 jit_solution(17442658351243271955)
XLA Ops:
  6.5 0.0 copy-start
  6.5 0.0 copy-start.1
  6.5 0.0 copy-start.2
  6.5 0.0 reduce-scatter.2.cloned.1.call-start
  6.5 5.8 %fusion = f32[512,64]{0,1:T(8,128)S(1)} fusion(bf16[64,7168]{1,0:T(8,128)(2,1)} %param.8, bf16[1,512,7168]{2,1,0:T(8,128)(2,1)} %param.6), kind=kOutput, calls=%fused_computation | convolution fusion | flops 469762048 | bytes 8388608 | tf_op jit(solution)/shard_map/dot_general | solution.py:25
  12.3 0.0 copy-done
  12.3 0.0 copy-done.1
  12.3 0.8 %fusion.2 = f32[512,64]{0,1:T(8,128)S(1)} fusion(bf16[64,2048]{1,0:T(8,128)(2,1)S(1)} %copy-done.1, bf16[1,512,2048]{2,1,0:T(8,128)(2,1)S(1)} %copy-done), kind=kOutput, calls=%fused_computation.2 | convolution fusion | flops 134217728 | bytes 2490368 | tf_op jit(solution)/shard_map/dot_general | solution.py:26
  13.1 0.7 %pad_maximum_fusion = f32[512,128]{0,1:T(8,128)} fusion(f32[512,64]{0,1:T(8,128)S(1)} %fusion.2, f32[512,64]{0,1:T(8,128)S(1)} %fusion), kind=kLoop, calls=%fused_computation.6 | loop fusion | flops 65536 | bytes 524288 | tf_op jit(solution)/shard_map/concatenate | solution.py:28
  13.8 0.0 reduce-scatter.2.cloned.1.call-update
  13.8 0.0 copy-done.2
  13.8 0.1 copy.9
  14.5 15.6 %all_gather.7 = bf16[1,16,4096]{2,0,1:T(2,128)(2,1)S(1)} all-gather(bf16[1,4,4096]{2,0,1:T(2,128)(2,1)S(1)} %copy.9), channel_id=1, replica_groups=mesh['ckpt'=2,'train'=4,'tensor'=4] {'train'}, dimensions={1}, use_global_device_ids=true | all-gather | bytes 163840 | tf_op jit(solution)/shard_map/all_gather | solution.py:37
  30.2 6.5 %reduce-scatter.2.cloned.1.call-done = f32[128,128]{0,1:T(8,128)} async-done(((f32[512,128]{0,1:T(8,128)}), f32[128,128]{0,1:T(8,128)}) %reduce-scatter.2.cloned.1.call-update) | async-done | bytes 65552 | tf_op jit(solution)/shard_map/reduce_scatter | solution.py:27
  36.7 1.0 %convolution_convert_fusion = bf16[64,64]{1,0:T(8,128)(2,1)S(1)} fusion(f32[1,128,128]{1,2,0:T(8,128)} %bitcast.22), kind=kOutput, calls=%fused_computation.4 | convolution fusion | flops 6295552 | bytes 73728 | tf_op jit(solution)/shard_map/sto,sti->soi/dot_general | solution.py:16
  37.7 0.1 reshape.35
  37.8 5.2 %all-gather = bf16[4,1,4096]{2,1,0:T(2,128)(2,1)S(1)} all-gather(bf16[1,1,4096]{2,1,0:T(2,128)(2,1)S(1)} %reshape.35), channel_id=1, replica_groups=mesh['ckpt'=2,'train'=4,'tensor'=4] {'tensor'}, dimensions={0}, use_global_device_ids=true | all-gather | bytes 40960 | tf_op jit(solution)/shard_map/all_gather | solution.py:31
  43.0 0.3 convolution_multiply_fusion
  43.3 0.1 reshape.34
  43.4 5.6 %psum.7 = f32[4,4,4]{2,1,0:T(4,128)} all-reduce(f32[4,4,4]{2,1,0:T(4,128)S(1)} %reshape.34), channel_id=1, replica_groups=mesh['ckpt'=2,'train'=4,'tensor'=4] {'ckpt'}, use_global_device_ids=true, to_apply=%region_1.0 | all-reduce | flops 64 | bytes 512 | tf_op jit(solution)/shard_map/psum | solution.py:43
Async XLA Ops:
  6.5 5.8 %copy-start = (bf16[1,512,2048]{2,1,0:T(8,128)(2,1)S(1)}, bf16[1,512,2048]{2,1,0:T(8,128)(2,1)}, u32[]{:S(2)}) copy-start(bf16[1,512,2048]{2,1,0:T(8,128)(2,1)} %param.7) | copy-start | bytes 6291460
  6.5 5.8 %copy-start.1 = (bf16[64,2048]{1,0:T(8,128)(2,1)S(1)}, bf16[64,2048]{1,0:T(8,128)(2,1)}, u32[]{:S(2)}) copy-start(bf16[64,2048]{1,0:T(8,128)(2,1)} %param.9) | copy-start | bytes 786436
  6.5 7.3 %copy-start.2 = (bf16[1,4,4096]{2,1,0:T(4,128)(2,1)S(1)}, bf16[1,4,4096]{2,1,0:T(4,128)(2,1)}, u32[]{:S(2)}) copy-start(bf16[1,4,4096]{2,1,0:T(4,128)(2,1)} %param.10) | copy-start | bytes 98308
  6.5 30.2 %reduce-scatter.2.cloned.1.call-start = ((), (), s32[]{:S(2)}) async-start(), calls=%async_computation.1 | async-start | bytes 327680 | tf_op jit(solution)/shard_map/reduce_scatter | solution.py:27
Sparse Core Ops, SparseCore 0:
  13.9 22.7 reduce-scatter.1
where the time goes:
time: 56 us; the launch traced here: 55.8 us
  blocking collectives  26.4 us (47%)
  between operations  14.1 us (25%)
  matrix products  7.76 us (14%)
  waiting for transfers between devices  6.55 us (12%)
  other arithmetic  0.72 us (1%)
    all_gather x1, blocking collectives, body(): lax.all_gather(test_grads, 'train', axis=1, tiled=True)[0]  15.6 us
    reduce_scatter x1, waiting for transfers between devices, body(): lax.psum_scatter(jnp.concatenate([left, right], axis=1), 'tensor', scatte...  6.54 us
    dot_general x1, matrix products, body(): lax.dot_general(h_local, proj_in, contract, preferred_element_type=jnp.fl...  5.76 us
    psum x1, blocking collectives, body(): total = lax.psum(table * weight, 'ckpt')  5.56 us
    all_gather x1, blocking collectives, body(): train_block = lax.all_gather(own, 'tensor', axis=0, tiled=True)  5.23 us
  transfers between devices with their start and end apart: 1, of which 1 were waited for; matrix products, arithmetic and copies ran while one was open for 0% of the time, Pallas kernels for 0%

commit v1 on v0

--- a/solution.py
+++ b/solution.py
@@ -7,6 +7,27 @@
 KIN = 64
 KOUT = 64
 SEQ = 128
+
+
+def collect(shard, axis, dim):
+    size, index, extent = (lax.axis_size(axis), lax.axis_index(axis), shard.shape[dim])
+    upward = [(i, (i + 1) % size) for i in range(size)]
+    left = [(i, (i - 1) % size) for i in range(size)]
+    out = jnp.zeros((*shard.shape[:dim], size * extent, *shard.shape[dim + 1 :]), shard.dtype)
+    out = lax.dynamic_update_slice_in_dim(out, shard, index * extent, axis=dim)
+    from_left = from_right = shard
+    halfway = size // 2
+    for lap in range(1, halfway + 1):
+        from_left = lax.ppermute(from_left, axis, upward)
+        out = lax.dynamic_update_slice_in_dim(
+            out, from_left, (index - lap) % size * extent, axis=dim
+        )
+        if lap < size - halfway:
+            from_right = lax.ppermute(from_right, axis, left)
+            out = lax.dynamic_update_slice_in_dim(
+                out, from_right, (index + lap) % size * extent, axis=dim
+            )
+    return out
 
 
 def outer_grads(sides):
@@ -28,7 +49,7 @@
         jnp.concatenate([left, right], axis=1), "tensor", scatter_dimension=0, tiled=True
     )
     own = outer_grads(shared)
-    train_block = lax.all_gather(own, "tensor", axis=0, tiled=True)
+    train_block = collect(own, "tensor", 0)
     tests = test_grads[0]
     width = tests.shape[0]
     examples = train_block.shape[0]

time: 56 us -> 69.5 us (1.24)
  waiting for transfers between devices: 6.55 us -> 24.2 us
  blocking collectives: 26.4 us -> 19.8 us
  starting transfers between devices: 0.01 us -> 1.78 us
    reduce_scatter x1, waiting for transfers between devices: 6.54 us -> 22.9 us  [body(): lax.psum_scatter(jnp.concatenate([left, right], axis=1), 'tensor', scatte...]
    all_gather x1 -> x0, blocking collectives: 5.23 us -> none  [body(): train_block = lax.all_gather(own, 'tensor', axis=0, tiled=True)]
    ppermute x0 -> x3, starting transfers between devices: none -> 1.78 us  [the longest x1 1.77 us: collect(): from_right = lax.ppermute(from_right, axis, left)]
    all_gather x1, blocking collectives: 15.6 us -> 14.2 us  [body(): lax.all_gather(test_grads, 'train', axis=1, tiled=True)[0]]
    ppermute x0 -> x3, waiting for transfers between devices: none -> 1.31 us  [the longest x2 1.31 us: collect(): from_left = lax.ppermute(from_left, axis, upward)]
  transfers between devices with their start and end apart: 1 -> 4, of which waited for: 1 -> 2; matrix products, arithmetic and copies ran while one was open for 0% -> 1% of each run, Pallas kernels for 0% -> 0%
where the time goes in v1:
time: 69.5 us; the launch traced here: 69.3 us
  waiting for transfers between devices  24.2 us (35%)
  blocking collectives  19.8 us (28%)
  between operations  14.2 us (20%)
  matrix products  7.74 us (11%)
  starting transfers between devices  1.78 us (3%)
  local copies, waits for them, and re-layouts  0.88 us (1%)
  other arithmetic  0.71 us (1%)
    reduce_scatter x1, waiting for transfers between devices, body(): lax.psum_scatter(jnp.concatenate([left, right], axis=1), 'tensor', scatte...  22.9 us
    all_gather x1, blocking collectives, body(): lax.all_gather(test_grads, 'train', axis=1, tiled=True)[0]  14.2 us
    dot_general x1, matrix products, body(): lax.dot_general(h_local, proj_in, contract, preferred_element_type=jnp.fl...  5.76 us
    psum x1, blocking collectives, body(): total = lax.psum(table * weight, 'ckpt')  5.57 us
    ppermute x1, starting transfers between devices, collect(): from_right = lax.ppermute(from_right, axis, left)  1.77 us
  transfers between devices with their start and end apart: 4, of which 2 were waited for; matrix products, arithmetic and copies ran while one was open for 1% of the time, Pallas kernels for 0%

profile of v1, /device:TPU:0, one launch (start us, length us, event | category | flops | bytes accessed | tf_op | source)
XLA Modules:
  0.0 69.3 jit_solution(11364030979759713573)
XLA Ops:
  6.5 0.0 copy-start
  6.5 0.0 copy-start.1
  6.5 0.0 copy-start.2
  6.5 0.0 reduce-scatter.2.cloned.1.call-start
  6.5 5.8 %fusion = f32[512,64]{0,1:T(8,128)S(1)} fusion(bf16[64,7168]{1,0:T(8,128)(2,1)} %param.8, bf16[1,512,7168]{2,1,0:T(8,128)(2,1)} %param.6), kind=kOutput, calls=%fused_computation | convolution fusion | flops 469762048 | bytes 8388608 | tf_op jit(solution)/shard_map/dot_general | solution.py:46
  12.3 0.0 copy-done
  12.3 0.0 copy-done.1
  12.3 0.8 %fusion.2 = f32[512,64]{0,1:T(8,128)S(1)} fusion(bf16[64,2048]{1,0:T(8,128)(2,1)S(1)} %copy-done.1, bf16[1,512,2048]{2,1,0:T(8,128)(2,1)S(1)} %copy-done), kind=kOutput, calls=%fused_computation.2 | convolution fusion | flops 134217728 | bytes 2490368 | tf_op jit(solution)/shard_map/dot_general | solution.py:47
  13.1 0.7 %pad_maximum_fusion = f32[512,128]{0,1:T(8,128)} fusion(f32[512,64]{0,1:T(8,128)S(1)} %fusion.2, f32[512,64]{0,1:T(8,128)S(1)} %fusion), kind=kLoop, calls=%fused_computation.6 | loop fusion | flops 65536 | bytes 524288 | tf_op jit(solution)/shard_map/concatenate | solution.py:49
  13.8 0.0 reduce-scatter.2.cloned.1.call-update
  13.8 22.9 %reduce-scatter.2.cloned.1.call-done = f32[128,128]{0,1:T(8,128)} async-done(((f32[512,128]{0,1:T(8,128)}), f32[128,128]{0,1:T(8,128)}) %reduce-scatter.2.cloned.1.call-update) | async-done | bytes 65552 | tf_op jit(solution)/shard_map/reduce_scatter | solution.py:48
  36.7 1.0 %convolution_convert_fusion = bf16[64,64]{1,0:T(8,128)(2,1)S(1)} fusion(f32[1,128,128]{1,2,0:T(8,128)} %bitcast.20), kind=kOutput, calls=%fused_computation.4 | convolution fusion | flops 6295552 | bytes 73728 | tf_op jit(solution)/shard_map/sto,sti->soi/dot_general | solution.py:37
  37.7 0.1 convert_element_type.19
  37.8 0.0 collective-permute-start
  37.8 0.0 copy-done.2
  37.8 0.1 copy.8
  37.8 1.8 %collective-permute-start.1 = (bf16[1,4096]{1,0:T(2,128)(2,1)S(1)}, bf16[1,4096]{1,0:T(2,128)(2,1)S(1)}, u32[]{:S(2)}, u32[]{:S(2)}) collective-permute-start(bf16[1,4096]{1,0:T(2,128)(2,1)S(1)} %convert_element_type.19), channel_id=1, source_target_pairs={{0,3},{1,0},{2,1},{3,2},{4,7},{5,4},{6,5},{7,6},{8,11},{9,8},{10,9... | collective-permute-start | bytes 24584 | tf_op jit(solution)/shard_map/ppermute | solution.py:26
  39.6 1.3 %collective-permute-done = bf16[1,4096]{1,0:T(2,128)(2,1)S(1)} collective-permute-done((bf16[1,4096]{1,0:T(2,128)(2,1)S(1)}, bf16[1,4096]{1,0:T(2,128)(2,1)S(1)}, u32[]{:S(2)}, u32[]{:S(2)}) %collective-permute-start) | collective-permute-done | bytes 8224 | tf_op jit(solution)/shard_map/ppermute | solution.py:21
  40.9 0.0 collective-permute-start.2
  40.9 14.2 %all_gather.3 = bf16[1,16,4096]{2,0,1:T(2,128)(2,1)S(1)} all-gather(bf16[1,4,4096]{2,0,1:T(2,128)(2,1)S(1)} %copy.8), channel_id=1, replica_groups=mesh['ckpt'=2,'train'=4,'tensor'=4] {'train'}, dimensions={1}, use_global_device_ids=true | all-gather | bytes 163840 | tf_op jit(solution)/shard_map/all_gather | solution.py:58
  55.8 0.2 dynamic_update_slice.12
  56.0 0.2 dynamic_update_slice.13
  56.2 0.0 collective-permute-done.1
  56.2 0.2 dynamic_update_slice.14
  56.4 0.0 collective-permute-done.2
  56.4 0.2 dynamic_update_slice.15
  56.5 0.3 convolution_multiply_fusion
  56.8 0.1 reshape.34
  56.9 5.6 %psum.7 = f32[4,4,4]{2,1,0:T(4,128)} all-reduce(f32[4,4,4]{2,1,0:T(4,128)S(1)} %reshape.34), channel_id=1, replica_groups=mesh['ckpt'=2,'train'=4,'tensor'=4] {'ckpt'}, use_global_device_ids=true, to_apply=%region_1.2 | all-reduce | flops 64 | bytes 512 | tf_op jit(solution)/shard_map/psum | solution.py:64
  (1 shorter events, 0.0 us)
Async XLA Ops:
  6.5 5.8 %copy-start = (bf16[1,512,2048]{2,1,0:T(8,128)(2,1)S(1)}, bf16[1,512,2048]{2,1,0:T(8,128)(2,1)}, u32[]{:S(2)}) copy-start(bf16[1,512,2048]{2,1,0:T(8,128)(2,1)} %param.7) | copy-start | bytes 6291460
  6.5 5.8 %copy-start.1 = (bf16[64,2048]{1,0:T(8,128)(2,1)S(1)}, bf16[64,2048]{1,0:T(8,128)(2,1)}, u32[]{:S(2)}) copy-start(bf16[64,2048]{1,0:T(8,128)(2,1)} %param.9) | copy-start | bytes 786436
  6.5 31.2 %copy-start.2 = (bf16[1,4,4096]{2,1,0:T(4,128)(2,1)S(1)}, bf16[1,4,4096]{2,1,0:T(4,128)(2,1)}, u32[]{:S(2)}) copy-start(bf16[1,4,4096]{2,1,0:T(4,128)(2,1)} %param.10) | copy-start | bytes 98308
  6.5 30.2 %reduce-scatter.2.cloned.1.call-start = ((), (), s32[]{:S(2)}) async-start(), calls=%async_computation.1 | async-start | bytes 327680 | tf_op jit(solution)/shard_map/reduce_scatter | solution.py:48
  37.8 3.2 %collective-permute-start = (bf16[1,4096]{1,0:T(2,128)(2,1)S(1)}, bf16[1,4096]{1,0:T(2,128)(2,1)S(1)}, u32[]{:S(2)}, u32[]{:S(2)}) collective-permute-start(bf16[1,4096]{1,0:T(2,128)(2,1)S(1)} %convert_element_type.19), channel_id=1, source_target_pairs={{0,1},{1,2},{2,3},{3,0},{4,5},{5,6},{6,7},{7,4},{8,9},{9,10},{10,1... | collective-permute-start | bytes 24584 | tf_op jit(solution)/shard_map/ppermute | solution.py:21
  37.8 18.3 %collective-permute-start.1 = (bf16[1,4096]{1,0:T(2,128)(2,1)S(1)}, bf16[1,4096]{1,0:T(2,128)(2,1)S(1)}, u32[]{:S(2)}, u32[]{:S(2)}) collective-permute-start(bf16[1,4096]{1,0:T(2,128)(2,1)S(1)} %convert_element_type.19), channel_id=1, source_target_pairs={{0,3},{1,0},{2,1},{3,2},{4,7},{5,4},{6,5},{7,6},{8,11},{9,8},{10,9... | collective-permute-start | bytes 24584 | tf_op jit(solution)/shard_map/ppermute | solution.py:26
  40.9 15.4 %collective-permute-start.2 = (bf16[1,4096]{1,0:T(2,128)(2,1)S(1)}, bf16[1,4096]{1,0:T(2,128)(2,1)S(1)}, u32[]{:S(2)}, u32[]{:S(2)}) collective-permute-start(bf16[1,4096]{1,0:T(2,128)(2,1)S(1)} %collective-permute-done), channel_id=1, source_target_pairs={{0,1},{1,2},{2,3},{3,0},{4,5},{5,6},{6,7},{7,4},{8,9},{9,10},{10,1... | collective-permute-start | bytes 24584 | tf_op jit(solution)/shard_map/ppermute | solution.py:21
Sparse Core Ops, SparseCore 0:
  13.9 22.7 reduce-scatter.1
